TPU v7x, 512 devices: a whole 4x8x8 slice. The times are simulated.
512 devices in a mesh: pipe: 8 (over z), space: 64 (over x, y, core).
Axes of the slice: x: 4, y: 8, z: 8, core: 2. Of those that a mesh axis runs over, the one named last changes fastest.
Arguments:
- activations: bfloat16 [8, 2, 96, 256, 512], P('pipe', None, None, 'space'), may hold values from -6 to 6
- cotangent: bfloat16 [8, 2, 96, 256, 512], P('pipe', None, None, 'space'), may hold values from -6 to 6
- kept_modes: int32 [8, 2], P('pipe'), may hold values from 32 to 128, as said below
- weight_in: float32 [8, 2, 2, 96, 96], P('pipe'), may hold values from -0.4375 to 0.4375
- bias_in: float32 [8, 2, 2, 96], P('pipe'), may hold values from -4 to 4
- weight_out: float32 [8, 2, 2, 96, 96], P('pipe'), may hold values from -0.4375 to 0.4375
Outputs:
- grad_input: bfloat16 [8, 2, 96, 256, 512], P('pipe', None, None, 'space')
- grad_weight_in: float32 [8, 2, 2, 96, 96], P('pipe')
- grad_bias_in: float32 [8, 2, 2, 96], P('pipe')
- grad_weight_out: float32 [8, 2, 2, 96, 96], P('pipe')
- grad_bias_out: float32 [8, 2, 2, 96], P('pipe')
Inputs may be any that keep to these rules, and one draw needn't show every extreme that they name: `kept_modes`: column 0 is a layer's kept longitude wavenumbers, from 64 to 128, with exactly 128 in some layer; column 1 is the kept latitude wavenumbers of each sign, from 32 to 64, with exactly 64 in some layer.
All inputs are finite; a program needn't handle non-finite values.
Results may differ from a plain program's by a relative error of at most 0.001.
Values may be sent and summed in bfloat16 or wider, within the bound.
No kernel may reach another device: no remote copies, remote signals or barrier semaphores. Data moves between devices by JAX's collectives and lax.ppermute only.
A program may use at most 64 MiB of HBM per device.

v0:
```python
import math
import jax
import jax.numpy as jnp
from jax import lax
from jax.sharding import PartitionSpec as P

LAT = 256
LON = 512
KEEP_LON = 128
KEEP_LAT = 64
HIGHEST = lax.Precision.HIGHEST


def from_behind(block, axis, distance):
    devices = range(lax.axis_size(axis))
    route = [(i - distance, i) for i in devices if i - distance in devices]
    return lax.ppermute(block, axis, route)


def lon_tables(length, count):
    column = jnp.arange(length, dtype=jnp.int32)
    number = jnp.arange(count, dtype=jnp.int32)
    phase = column[:, None] * number[None, :] % length
    angle = phase.astype(jnp.float32) * (2.0 * math.pi / length)
    factor = 1.0 / math.sqrt(length)
    return (jnp.cos(angle) * factor, jnp.sin(angle) * factor)


def lat_tables(length, half):
    signed = jnp.arange(2 * half, dtype=jnp.int32) - half
    row_index = jnp.arange(length, dtype=jnp.int32)
    phase = signed[:, None] * row_index[None, :] % length
    angle = phase.astype(jnp.float32) * (2.0 * math.pi / length)
    factor = 1.0 / math.sqrt(length)
    return (jnp.cos(angle) * factor, jnp.sin(angle) * factor)


def lon_forward_table(cos_table, sin_table, ndev):
    share = cos_table.shape[1] // ndev
    cos_g = cos_table.reshape(-1, ndev, 1, share)
    sin_g = -sin_table.reshape(-1, ndev, 1, share)
    return jnp.concatenate([cos_g, sin_g], axis=2).reshape(cos_table.shape[0], -1)


def lon_forward(field, table):
    values = field.astype(jnp.float32)
    return jnp.einsum("ibln,nc->iblc", values, table, precision=HIGHEST)


def lat_forward(spectrum, cos_table, sin_table):
    top = jnp.stack([cos_table, sin_table], axis=1)
    bottom = jnp.stack([-sin_table, cos_table], axis=1)
    table = jnp.stack([top, bottom])
    return jnp.einsum("ofpl,iblpj->oibfj", table, spectrum, precision=HIGHEST)


def lat_inverse(spectrum, cos_table, sin_table):
    top = jnp.stack([cos_table, -sin_table])
    bottom = jnp.stack([sin_table, cos_table])
    table = jnp.stack([top, bottom])
    return jnp.einsum("opfl,pibfj->oiblj", table, spectrum, precision=HIGHEST)


def lon_inverse(spectrum, cos_table, sin_table):
    table = jnp.stack([cos_table, -sin_table])
    return jnp.einsum("piblk,pnk->ibln", spectrum, table, precision=HIGHEST)


def mode_mask(signed, wavenumber, keep_lon, keep_lat):
    lat_kept = (signed >= -keep_lat) & (signed < keep_lat)
    lon_kept = wavenumber < keep_lon
    factor = jnp.where(wavenumber == 0, 1.0, 2.0).astype(jnp.float32)
    return (lat_kept[:, None] & lon_kept[None, :]).astype(jnp.float32) * factor[None, :]


def block_product(weights, values):
    return jnp.einsum("kij,kjm->kim", weights, values, precision=HIGHEST)


def complex_apply(weights, values):
    real_part = block_product(weights[0], values[0]) - block_product(weights[1], values[1])
    imag_part = block_product(weights[1], values[0]) + block_product(weights[0], values[1])
    return jnp.stack([real_part, imag_part])


def complex_adjoint(weights, values):
    real_t = jnp.swapaxes(weights[0], 1, 2)
    imag_t = jnp.swapaxes(weights[1], 1, 2)
    real_part = block_product(real_t, values[0]) + block_product(imag_t, values[1])
    imag_part = block_product(real_t, values[1]) - block_product(imag_t, values[0])
    return jnp.stack([real_part, imag_part])


def complex_outer(left, right):

    def outer(first, second):
        return jnp.einsum("kim,kjm->kij", first, second, precision=HIGHEST)

    real_part = outer(left[0], right[0]) + outer(left[1], right[1])
    imag_part = outer(left[1], right[0]) - outer(left[0], right[1])
    return jnp.stack([real_part, imag_part])


def gelu_pair(values):
    inner = 0.7978845608 * (values + 0.044715 * values * values * values)
    tangent = jnp.tanh(inner)
    output = 0.5 * values * (1.0 + tangent)
    slope = 0.5 * (1.0 + tangent) + 0.5 * values * (1.0 - tangent * tangent) * 0.7978845608 * (
        1.0 + 3.0 * 0.044715 * values * values
    )
    return (output, slope)


def backprop(spectrum, grad_spec, weight_in, bias_in, weight_out):
    before = complex_apply(weight_in, spectrum) + bias_in[..., None]
    hidden, slope = gelu_pair(before)
    grad_hidden = complex_adjoint(weight_out, grad_spec)
    grad_before = grad_hidden * slope
    grad_modes = complex_adjoint(weight_in, grad_before)
    grad_w_out = complex_outer(grad_spec, hidden)
    grad_w_in = complex_outer(grad_before, spectrum)
    return (
        grad_modes,
        grad_w_in,
        jnp.sum(grad_before, axis=-1),
        grad_w_out,
        jnp.sum(grad_spec, axis=-1),
    )


def to_columns(spectrum, ndev):
    moved = lax.all_to_all(spectrum, "space", split_axis=3, concat_axis=2, tiled=True)
    nblocks, width, rows, _ = moved.shape
    return moved.reshape(nblocks, width, rows, 2, -1)


def shards(activations, cotangent, kept_modes, weight_in, bias_in, weight_out):
    field = activations[0]
    own_grad = cotangent[0]
    nblocks = field.shape[0]
    width = field.shape[1]
    ndev = lax.axis_size("space")
    received = from_behind(own_grad, "pipe", -1)
    section_index = lax.axis_index("pipe")
    last_section = lax.axis_size("pipe") - 1
    upstream = jnp.where(section_index == last_section, own_grad, received)
    lon_cos, lon_sin = lon_tables(LON, KEEP_LON)
    lat_cos, lat_sin = lat_tables(LAT, KEEP_LAT)
    table = lon_forward_table(lon_cos, lon_sin, ndev)
    col_field = to_columns(lon_forward(field, table), ndev)
    col_grad = to_columns(lon_forward(upstream, table), ndev)
    spectrum = lat_forward(col_field, lat_cos, lat_sin)
    grad_spec = lat_forward(col_grad, lat_cos, lat_sin)
    share = KEEP_LON // ndev
    signed = jnp.arange(2 * KEEP_LAT, dtype=jnp.int32) - KEEP_LAT
    wavenumber = lax.axis_index("space") * share + jnp.arange(share, dtype=jnp.int32)
    weight = mode_mask(signed, wavenumber, kept_modes[0, 0], kept_modes[0, 1])
    grad_spec = grad_spec * weight
    spectrum = spectrum.reshape(2, nblocks, width, -1)
    grad_spec = grad_spec.reshape(2, nblocks, width, -1)
    grad_modes, grad_w_in, grad_b_in, grad_w_out, grad_b_out = backprop(
        spectrum, grad_spec, weight_in[0], bias_in[0], weight_out[0]
    )
    grad_modes = grad_modes.reshape(2, nblocks, width, 2 * KEEP_LAT, share)
    lat_back = lat_inverse(grad_modes, lat_cos, lat_sin)
    rows_back = lax.all_to_all(lat_back, "space", split_axis=3, concat_axis=4, tiled=True)
    inverse = lon_inverse(rows_back, lon_cos, lon_sin)
    parts = (grad_w_in, grad_b_in, grad_w_out, grad_b_out)
    flat = lax.psum(jnp.concatenate([p.reshape(-1) for p in parts]), "space")
    factor = 1.0 / math.sqrt(2 * KEEP_LAT * KEEP_LON)
    flat = flat * factor
    sums = []
    start = 0
    for p in parts:
        sums.append(flat[start : start + p.size].reshape(p.shape)[None])
        start += p.size
    grad_field = (upstream.astype(jnp.float32) + inverse).astype(jnp.bfloat16)
    return (grad_field[None], *sums)


def solution(mesh):
    return jax.shard_map(
        shards,
        mesh=mesh,
        in_specs=(
            P("pipe", None, None, "space", None),
            P("pipe", None, None, "space", None),
            P("pipe", None),
            P("pipe", None, None, None, None),
            P("pipe", None, None, None),
            P("pipe", None, None, None, None),
        ),
        out_specs=(
            P("pipe", None, None, "space", None),
            P("pipe", None, None, None, None),
            P("pipe", None, None, None),
            P("pipe", None, None, None, None),
            P("pipe", None, None, None),
        ),
        check_vma=False,
    )
```

profile of v0, /device:TPU:1, one launch (start us, length us, event | category | flops | bytes accessed | tf_op | source)
XLA Modules:
  0.0 321.6 jit_solution(10139144057353818044)
XLA Ops:
  7.2 2.2 copy.270
  13.5 1.3 copy.181
  14.9 11.6 %all-to-all-start.1 = ((f32[2,96,4,256]{1,2,0,3:T(4,128)}), f32[2,96,4,256]{1,2,0,3:T(4,128)S(1)}, u32[]{:S(2)}, u32[]{:S(2)}) async-start(f32[2,96,4,256]{1,2,0,3:T(4,128)} %copy.181), calls=%async_computation.1 | async-start | bytes 2097152 | tf_op jit(solution)/shard_map/all_to_all | solution.py:132
  28.4 1.8 multiply_negate_fusion
  31.6 1.3 fusion.92
  32.9 1.7 broadcast_select_fusion
  34.6 1.7 fusion.16
  36.3 2.5 copy.167
  38.8 16.3 %all-to-all-done.1 = f32[2,96,4,256]{1,2,0,3:T(4,128)S(1)} async-done(((f32[2,96,4,256]{1,2,0,3:T(4,128)}), f32[2,96,4,256]{1,2,0,3:T(4,128)S(1)}, u32[]{:S(2)}, u32[]{:S(2)}) %all-to-all-start.1) | async-done | bytes 786464 | tf_op jit(solution)/shard_map/all_to_all | solution.py:132
  55.1 6.4 %all-to-all-start = ((f32[2,96,4,256]{1,2,0,3:T(4,128)}), f32[2,96,4,256]{1,2,0,3:T(4,128)}, u32[]{:S(2)}, u32[]{:S(2)}) async-start(f32[2,96,4,256]{1,2,0,3:T(4,128)} %copy.167), calls=%async_computation | async-start | bytes 2097152 | tf_op jit(solution)/shard_map/all_to_all | solution.py:132
  64.4 1.8 convolution_bitcast_fusion.2
  69.7 20.2 %all-to-all-done = f32[2,96,4,256]{1,2,0,3:T(4,128)} async-done(((f32[2,96,4,256]{1,2,0,3:T(4,128)}), f32[2,96,4,256]{1,2,0,3:T(4,128)}, u32[]{:S(2)}, u32[]{:S(2)}) %all-to-all-start) | async-done | bytes 786464 | tf_op jit(solution)/shard_map/all_to_all | solution.py:132
  89.9 1.4 copy.168
  92.1 2.5 fusion.105
  96.6 2.1 fusion.98
  104.8 1.7 fusion.9
  106.5 1.5 fusion.8
  110.5 1.3 fusion.3
  113.5 1.7 convolution_bitcast_fusion
  115.2 1.3 copy.199
  116.6 6.2 %all-to-all-start.2 = ((f32[2,2,96,256,2]{2,0,4,1,3:T(2,128)}), f32[2,2,96,256,2]{2,0,4,1,3:T(2,128)S(1)}, u32[]{:S(2)}, u32[]{:S(2)}) async-start(f32[2,2,96,256,2]{2,0,4,1,3:T(2,128)} %copy.199), calls=%async_computation.2 | async-start | bytes 2097152 | tf_op jit(solution)/shard_map/all_to_all | solution.py:166
  122.8 181.5 %all-reduce.2.cloned.1.call-done = f32[74496]{0:T(1024)} async-done(((f32[74496]{0:T(1024)}), f32[74496]{0:T(1024)}) %all-reduce.2.cloned.1.call-update) | async-done | bytes 298000 | tf_op jit(solution)/shard_map/psum | solution.py:169
  309.4 3.5 %fusion.20 = f32[2,96,4,512,1]{3,1,2,0,4:T(8,128)S(1)} fusion(f32[2,2,96,4,128]{2,4,3,1,0:T(8,128)S(1)} %bitcast.215, f32[1,512,128]{2,1,0:T(8,128)S(1)} %copy-done.5, f32[1,512,128]{2,1,0:T(8,128)S(1)} %copy-done.6), kind=kOutput, calls=%fused_computation.43 | convolution fusion | flops 1208090624 | bytes 2883584 | tf_op jit(solution)/shard_map/piblk,pnk->ibln/dot_general | solution.py:66
  313.2 1.5 copy.212
  (98 shorter events, 31.2 us)
Async XLA Ops:
  7.2 5.5 %copy-start = (bf16[1,2,96,4,512]{4,3,2,1,0:T(4,128)(2,1)S(1)}, bf16[1,2,96,4,512]{4,3,2,1,0:T(4,128)(2,1)}, u32[]{:S(2)}) copy-start(bf16[1,2,96,4,512]{4,3,2,1,0:T(4,128)(2,1)} %param.6) | copy-start | bytes 2359300
  9.4 23.5 %collective-permute-start = (bf16[2,96,4,512]{3,1,0,2:T(8,128)(2,1)}, bf16[2,96,4,512]{3,1,0,2:T(8,128)(2,1)}, u32[]{:S(2)}, u32[]{:S(2)}) collective-permute-start(bf16[2,96,4,512]{3,1,0,2:T(8,128)(2,1)} %bitcast.197), channel_id=1, source_target_pairs={{64,0},{128,64},{192,128},{256,192},{320,256},{384,320},{448,384},... | collective-permute-start | bytes 2359304 | tf_op jit(solution)/shard_map/ppermute | solution.py:17
  13.5 13.0 %copy-start.14 = (s32[1,2]{1,0:T(1,128)S(1)}, s32[1,2]{1,0:T(1,128)}, u32[]{:S(2)}) copy-start(s32[1,2]{1,0:T(1,128)} %param.8) | copy-start | bytes 28
  14.9 40.2 %all-to-all-start.1 = ((f32[2,96,4,256]{1,2,0,3:T(4,128)}), f32[2,96,4,256]{1,2,0,3:T(4,128)S(1)}, u32[]{:S(2)}, u32[]{:S(2)}) async-start(f32[2,96,4,256]{1,2,0,3:T(4,128)} %copy.181), calls=%async_computation.1 | async-start | bytes 2097152 | tf_op jit(solution)/shard_map/all_to_all | solution.py:132
  36.3 26.1 %copy-start.11 = (f32[1,128,256]{2,1,0:T(8,128)S(1)}, f32[1,128,256]{2,1,0:T(8,128)}, u32[]{:S(2)}) copy-start(f32[1,128,256]{2,1,0:T(8,128)} %get-tuple-element.53) | copy-start | bytes 393220
  36.3 26.1 %copy-start.12 = (f32[1,128,256]{2,1,0:T(8,128)S(1)}, f32[1,128,256]{2,1,0:T(8,128)}, u32[]{:S(2)}) copy-start(f32[1,128,256]{2,1,0:T(8,128)} %get-tuple-element.54) | copy-start | bytes 393220
  55.1 34.9 %all-to-all-start = ((f32[2,96,4,256]{1,2,0,3:T(4,128)}), f32[2,96,4,256]{1,2,0,3:T(4,128)}, u32[]{:S(2)}, u32[]{:S(2)}) async-start(f32[2,96,4,256]{1,2,0,3:T(4,128)} %copy.167), calls=%async_computation | async-start | bytes 2097152 | tf_op jit(solution)/shard_map/all_to_all | solution.py:132
  61.5 242.8 %all-reduce.2.cloned.1.call-start = ((), (), s32[]{:S(2)}) async-start(), calls=%async_computation.3 | async-start | bytes 598016 | tf_op jit(solution)/shard_map/psum | solution.py:169
  63.5 1.0 copy-start.4
  64.4 2.2 copy-start.1
  92.1 2.9 copy-start.10
  94.8 1.8 copy-start.13
  96.6 5.3 %copy-start.2 = (f32[1,2,2,96,96]{4,3,2,1,0:T(8,128)S(1)}, f32[1,2,2,96,96]{4,3,2,1,0:T(8,128)}, u32[]{:S(2)}) copy-start(f32[1,2,2,96,96]{4,3,2,1,0:T(8,128)} %param.9) | copy-start | bytes 442372
  104.6 5.9 %copy-start.3 = (f32[1,2,2,96,96]{4,3,2,1,0:T(8,128)S(1)}, f32[1,2,2,96,96]{4,3,2,1,0:T(8,128)}, u32[]{:S(2)}) copy-start(f32[1,2,2,96,96]{4,3,2,1,0:T(8,128)} %param.9) | copy-start | bytes 442372
  108.0 4.8 %copy-start.9 = (f32[2,256,96]{1,2,0:T(8,128)S(1)}, f32[2,256,96]{1,2,0:T(8,128)}, u32[]{:S(2)}) copy-start(f32[2,256,96]{1,2,0:T(8,128)} %fusion.50) | copy-start | bytes 589828
  110.5 3.0 copy-start.7
  110.5 3.0 copy-start.8
  116.6 191.6 %all-to-all-start.2 = ((f32[2,2,96,256,2]{2,0,4,1,3:T(2,128)}), f32[2,2,96,256,2]{2,0,4,1,3:T(2,128)S(1)}, u32[]{:S(2)}, u32[]{:S(2)}) async-start(f32[2,2,96,256,2]{2,0,4,1,3:T(2,128)} %copy.199), calls=%async_computation.2 | async-start | bytes 2097152 | tf_op jit(solution)/shard_map/all_to_all | solution.py:166
  308.4 1.0 copy-start.5
  308.4 1.0 copy-start.6
Sparse Core Ops, SparseCore 0:
  110.6 193.5 all-reduce.1
where the time goes:
time: 322 us
  waiting for transfers between devices  218 us (68%)
  matrix products  27.7 us (9%)
  starting transfers between devices  25.7 us (8%)
  local copies, waits for them, and re-layouts  21.3 us (7%)
  between operations  15.2 us (5%)
  other arithmetic  13.7 us (4%)
    psum x1, waiting for transfers between devices, shards(): flat = lax.psum(jnp.concatenate([p.reshape(-1) for p in parts]), 'space')  181 us
    all_to_all x2, waiting for transfers between devices, to_columns(): lax.all_to_all(spectrum, 'space', split_axis=3, concat_axis=2, tiled=True)  36.5 us
    all_to_all x2, starting transfers between devices, to_columns(): lax.all_to_all(spectrum, 'space', split_axis=3, concat_axis=2, tiled=True)  18 us
    dot_general x12, matrix products, block_product(): return jnp.einsum('kij,kjm->kim', weights, values, precision=HIGHEST)  8.45 us
    dot_general x8, matrix products, outer(): return jnp.einsum('kim,kjm->kij', first, second, precision=HIGHEST)  7.06 us
  transfers between devices with their start and end apart: 5, of which 3 were waited for; matrix products, arithmetic and copies ran while one was open for 10% of the time, Pallas kernels for 0%

commit v1 on v0

--- a/solution.py
+++ b/solution.py
@@ -166,7 +166,7 @@
     rows_back = lax.all_to_all(lat_back, "space", split_axis=3, concat_axis=4, tiled=True)
     inverse = lon_inverse(rows_back, lon_cos, lon_sin)
     parts = (grad_w_in, grad_b_in, grad_w_out, grad_b_out)
-    flat = lax.psum(jnp.concatenate([p.reshape(-1) for p in parts]), "space")
+    flat = jnp.sum(lax.all_gather(jnp.concatenate([p.reshape(-1) for p in parts]), "space"), axis=0)
     factor = 1.0 / math.sqrt(2 * KEEP_LAT * KEEP_LON)
     flat = flat * factor
     sums = []

time: 322 us -> 256 us (0.80)
  waiting for transfers between devices: 218 us -> 141 us
  other arithmetic: 13.7 us -> 23.3 us
  starting transfers between devices: 25.7 us -> 30.6 us
    psum x1 -> x0, waiting for transfers between devices: 181 us -> none  [shards(): flat = lax.psum(jnp.concatenate([p.reshape(-1) for p in parts]), 'space')]
    all_gather x0 -> x1, waiting for transfers between devices: none -> 65.4 us  [shards(): lax.all_gather(jnp.concatenate([p.reshape(-1) for p in parts]), 'space')]
    all_to_all x1, waiting for transfers between devices: 0.01 us -> 36.6 us  [shards(): lax.all_to_all(lat_back, 'space', split_axis=3, concat_axis=4, tiled=True)]
    ppermute x1, waiting for transfers between devices: 0.01 us -> 18 us  [from_behind(): return lax.ppermute(block, axis, route)]
    all_to_all x2, waiting for transfers between devices: 36.5 us -> 21.3 us  [to_columns(): lax.all_to_all(spectrum, 'space', split_axis=3, concat_axis=2, tiled=True)]
    reduce_sum x0 -> x1, other arithmetic: none -> 14.7 us  [shards(): jnp.sum(lax.all_gather(jnp.concatenate([p.reshape(-1) for p in parts]), '...]
    all_to_all x2, starting transfers between devices: 18 us -> 22.9 us  [to_columns(): lax.all_to_all(spectrum, 'space', split_axis=3, concat_axis=2, tiled=True)]
  transfers between devices with their start and end apart: 5 -> 5, of which waited for: 3 -> 4; matrix products, arithmetic and copies ran while one was open for 10% -> 11% of each run, Pallas kernels for 0% -> 0%
where the time goes in v1:
time: 256 us
  waiting for transfers between devices  141 us (55%)
  starting transfers between devices  30.6 us (12%)
  matrix products  26.1 us (10%)
  other arithmetic  23.3 us (9%)
  local copies, waits for them, and re-layouts  19.1 us (7%)
  between operations  15.2 us (6%)
    all_gather x1, waiting for transfers between devices, shards(): lax.all_gather(jnp.concatenate([p.reshape(-1) for p in parts]), 'space')  65.4 us
    all_to_all x1, waiting for transfers between devices, shards(): lax.all_to_all(lat_back, 'space', split_axis=3, concat_axis=4, tiled=True)  36.6 us
    all_to_all x2, starting transfers between devices, to_columns(): lax.all_to_all(spectrum, 'space', split_axis=3, concat_axis=2, tiled=True)  22.9 us
    all_to_all x2, waiting for transfers between devices, to_columns(): lax.all_to_all(spectrum, 'space', split_axis=3, concat_axis=2, tiled=True)  21.3 us
    ppermute x1, waiting for transfers between devices, from_behind(): return lax.ppermute(block, axis, route)  18 us
    reduce_sum x1, other arithmetic, shards(): jnp.sum(lax.all_gather(jnp.concatenate([p.reshape(-1) for p in parts]), '...  14.7 us
    dot_general x8, matrix products, outer(): return jnp.einsum('kim,kjm->kij', first, second, precision=HIGHEST)  8.4 us
    all_to_all x1, starting transfers between devices, shards(): lax.all_to_all(lat_back, 'space', split_axis=3, concat_axis=4, tiled=True)  6.19 us
  transfers between devices with their start and end apart: 5, of which 4 were waited for; matrix products, arithmetic and copies ran while one was open for 11% of the time, Pallas kernels for 0%

profile of v1, /device:TPU:1, one launch (start us, length us, event | category | flops | bytes accessed | tf_op | source)
XLA Modules:
  0.0 255.6 jit_solution(3613578228125817604)
XLA Ops:
  10.0 1.3 copy.181
  11.4 11.8 %all-to-all-start.1 = ((f32[2,96,4,256]{1,2,0,3:T(4,128)}), f32[2,96,4,256]{1,2,0,3:T(4,128)S(1)}, u32[]{:S(2)}, u32[]{:S(2)}) async-start(f32[2,96,4,256]{1,2,0,3:T(4,128)} %copy.181), calls=%async_computation.1 | async-start | bytes 2097152 | tf_op jit(solution)/shard_map/all_to_all | solution.py:132
  24.2 1.3 collective-permute-start
  28.0 18.0 %collective-permute-done = bf16[2,96,4,512]{3,1,0,2:T(8,128)(2,1)} collective-permute-done((bf16[2,96,4,512]{3,1,0,2:T(8,128)(2,1)}, bf16[2,96,4,512]{3,1,0,2:T(8,128)(2,1)}, u32[]{:S(2)}, u32[]{:S(2)}) %collective-permute-start) | collective-permute-done | bytes 786464 | tf_op jit(solution)/shard_map/ppermute | solution.py:17
  46.0 1.7 broadcast_select_fusion
  47.6 1.7 fusion.16
  49.4 2.5 copy.167
  51.8 11.1 %all-to-all-start = ((f32[2,96,4,256]{1,2,0,3:T(4,128)}), f32[2,96,4,256]{1,2,0,3:T(4,128)}, u32[]{:S(2)}, u32[]{:S(2)}) async-start(f32[2,96,4,256]{1,2,0,3:T(4,128)} %copy.167), calls=%async_computation | async-start | bytes 2097152 | tf_op jit(solution)/shard_map/all_to_all | solution.py:132
  64.9 1.8 convolution_bitcast_fusion.2
  70.1 21.3 %all-to-all-done = f32[2,96,4,256]{1,2,0,3:T(4,128)} async-done(((f32[2,96,4,256]{1,2,0,3:T(4,128)}), f32[2,96,4,256]{1,2,0,3:T(4,128)}, u32[]{:S(2)}, u32[]{:S(2)}) %all-to-all-start) | async-done | bytes 786464 | tf_op jit(solution)/shard_map/all_to_all | solution.py:132
  91.4 1.4 copy.168
  93.6 1.9 fusion.105
  97.5 1.5 fusion.98
  99.0 1.3 fusion.45
  102.9 1.5 fusion.8
  104.4 1.5 fusion.9
  112.5 1.7 convolution_bitcast_fusion
  114.2 1.3 copy.199
  115.5 6.2 %all-to-all-start.2 = ((f32[2,2,96,256,2]{2,0,4,1,3:T(2,128)}), f32[2,2,96,256,2]{2,0,4,1,3:T(2,128)S(1)}, u32[]{:S(2)}, u32[]{:S(2)}) async-start(f32[2,2,96,256,2]{2,0,4,1,3:T(2,128)} %copy.199), calls=%async_computation.2 | async-start | bytes 2097152 | tf_op jit(solution)/shard_map/all_to_all | solution.py:166
  122.8 36.6 %all-to-all-done.2 = f32[2,2,96,256,2]{2,0,4,1,3:T(2,128)S(1)} async-done(((f32[2,2,96,256,2]{2,0,4,1,3:T(2,128)}), f32[2,2,96,256,2]{2,0,4,1,3:T(2,128)S(1)}, u32[]{:S(2)}, u32[]{:S(2)}) %all-to-all-start.2) | async-done | bytes 786464 | tf_op jit(solution)/shard_map/all_to_all | solution.py:166
  160.4 3.5 %fusion.20 = f32[2,96,4,512,1]{3,1,2,0,4:T(8,128)S(1)} fusion(f32[2,2,96,4,128]{2,4,3,1,0:T(8,128)S(1)} %bitcast.215, f32[1,512,128]{2,1,0:T(8,128)S(1)} %get-tuple-element.57, f32[1,512,128]{2,1,0:T(8,128)S(1)} %get-tuple-element.58), kind=kOutput, calls=%fused_computation.43 | convolution fusion | flops 1208090624 | bytes 2883584 | tf_op jit(solution)/shard_map/piblk,pnk->ibln/dot_general | solution.py:66
  164.2 1.5 copy.212
  165.7 65.4 %all-gather.4.cloned.1.call-done = f32[64,1,74496]{2,1,0:T(1,128)} async-done(((f32[1,1,74496]{2,1,0:T(1,128)}), f32[64,1,74496]{2,1,0:T(1,128)}) %all-gather.4.cloned.1.call-update) | async-done | bytes 19070992 | tf_op jit(solution)/shard_map/all_gather | solution.py:169
  231.1 14.7 %reduce_sum.29 = f32[74496]{0:T(1024)S(1)} reduce(f32[64,1,74496]{2,1,0:T(1,128)} %all-gather.4.cloned.1.call-done, f32[]{:T(128)} %constant.76.clone.1), dimensions={0,1}, to_apply=%region_2.3 | reduce | flops 4693248 | bytes 19368964 | tf_op jit(solution)/shard_map/reduce_sum | solution.py:169
  (84 shorter events, 28.0 us)
Async XLA Ops:
  7.2 2.0 copy-start
  10.0 13.1 %copy-start.1 = (bf16[1,2,96,4,512]{4,3,2,1,0:T(4,128)(2,1)S(1)}, bf16[1,2,96,4,512]{4,3,2,1,0:T(4,128)(2,1)}, u32[]{:S(2)}) copy-start(bf16[1,2,96,4,512]{4,3,2,1,0:T(4,128)(2,1)} %param.7) | copy-start | bytes 2359300
  11.4 14.1 %copy-start.6 = (s32[1,2]{1,0:T(1,128)S(1)}, s32[1,2]{1,0:T(1,128)}, u32[]{:S(2)}) copy-start(s32[1,2]{1,0:T(1,128)} %param.8) | copy-start | bytes 28
  11.4 40.5 %all-to-all-start.1 = ((f32[2,96,4,256]{1,2,0,3:T(4,128)}), f32[2,96,4,256]{1,2,0,3:T(4,128)S(1)}, u32[]{:S(2)}, u32[]{:S(2)}) async-start(f32[2,96,4,256]{1,2,0,3:T(4,128)} %copy.181), calls=%async_computation.1 | async-start | bytes 2097152 | tf_op jit(solution)/shard_map/all_to_all | solution.py:132
  24.2 21.8 %collective-permute-start = (bf16[2,96,4,512]{3,1,0,2:T(8,128)(2,1)}, bf16[2,96,4,512]{3,1,0,2:T(8,128)(2,1)}, u32[]{:S(2)}, u32[]{:S(2)}) collective-permute-start(bf16[2,96,4,512]{3,1,0,2:T(8,128)(2,1)} %bitcast.197), channel_id=1, source_target_pairs={{64,0},{128,64},{192,128},{256,192},{320,256},{384,320},{448,384},... | collective-permute-start | bytes 2359304 | tf_op jit(solution)/shard_map/ppermute | solution.py:17
  51.8 39.6 %all-to-all-start = ((f32[2,96,4,256]{1,2,0,3:T(4,128)}), f32[2,96,4,256]{1,2,0,3:T(4,128)}, u32[]{:S(2)}, u32[]{:S(2)}) async-start(f32[2,96,4,256]{1,2,0,3:T(4,128)} %copy.167), calls=%async_computation | async-start | bytes 2097152 | tf_op jit(solution)/shard_map/all_to_all | solution.py:132
  63.0 168.1 %all-gather.4.cloned.1.call-start = ((), (), s32[]{:S(2)}) async-start(), calls=%async_computation.3 | async-start | bytes 19368960 | tf_op jit(solution)/shard_map/all_gather | solution.py:169
  64.9 2.2 copy-start.2
  93.6 2.3 copy-start.4
  95.7 1.8 copy-start.5
  108.0 1.8 copy-start.3
  115.5 43.9 %all-to-all-start.2 = ((f32[2,2,96,256,2]{2,0,4,1,3:T(2,128)}), f32[2,2,96,256,2]{2,0,4,1,3:T(2,128)S(1)}, u32[]{:S(2)}, u32[]{:S(2)}) async-start(f32[2,2,96,256,2]{2,0,4,1,3:T(2,128)} %copy.199), calls=%async_computation.2 | async-start | bytes 2097152 | tf_op jit(solution)/shard_map/all_to_all | solution.py:166
Sparse Core Ops, SparseCore 0:
  109.2 121.7 all-gather.3
